TPU v7x, 32 devices: a whole 2x2x4 slice. The times are simulated.
32 devices in a mesh: grp: 2 (over y), outer: 4 (over x, core), inner: 4 (over z).
Axes of the slice: x: 2, y: 2, z: 4, core: 2. Of those that a mesh axis runs over, the one named last changes fastest.
Arguments:
- query: bfloat16 [4096, 1024], P(('grp', 'outer', 'inner')), parts along dimension 0, may hold values from -6 to 6
- key: bfloat16 [4096, 1024], P(('grp', 'outer', 'inner')), parts along dimension 0, may hold values from -6 to 6
- value: bfloat16 [4096, 1024], P(('grp', 'outer', 'inner')), parts along dimension 0, may hold values from -6 to 6
- grad_out: bfloat16 [4096, 1024], P(('grp', 'outer', 'inner')), parts along dimension 0, may hold values from -6 to 6
Outputs:
- normed_out: bfloat16 [4096, 1024], P(('grp', 'outer', 'inner')), parts along dimension 0
- grad_query: bfloat16 [4096, 1024], P(('grp', 'outer', 'inner')), parts along dimension 0
- grad_key: bfloat16 [4096, 1024], P(('grp', 'outer', 'inner')), parts along dimension 0
- grad_value: bfloat16 [4096, 1024], P(('grp', 'outer', 'inner')), parts along dimension 0
There are 2 independent parts, one for each index of `grp`. A program takes and returns all parts, laid end to end along the dimension named above; each array names one. Nothing has to cross between parts.
All inputs are finite; a program needn't handle non-finite values.
Results may differ from a plain program's by a relative error of at most 0.0059.
Values sent between devices are 32-bit elements; how exact they have to be, the bound alone decides.
No kernel may reach another device: no remote copies, remote signals or barrier semaphores. Data moves between devices by JAX's collectives and lax.ppermute only.
A program may use at most 64 MiB of HBM per device.

v0:
```python
import jax
import jax.numpy as jnp
from jax import lax
from jax.sharding import PartitionSpec as P

HEADS = 8
HEAD = 128


def carried_in(value, axis, join, neutral, backward):
    count, mine = (lax.axis_size(axis), lax.axis_index(axis))
    pieces = lax.all_gather(value, axis)
    if backward:
        pieces = pieces[::-1]
        mine = count - 1 - mine
    running = jnp.full_like(value, 0) + jnp.asarray(neutral, value.dtype)

    def lap(position, running):
        longer = join(running, pieces[position])
        return jnp.where(position < mine, longer, running)

    return lax.fori_loop(0, count - 1, lap, running)


def add_terms(earlier, later):
    return earlier + later


def forward_prefix(state):
    empty_state = jnp.zeros_like(state)
    inner_prior = carried_in(state, "inner", add_terms, empty_state, False)
    row_total = lax.psum(state, "inner")
    return carried_in(row_total, "outer", add_terms, empty_state, False) + inner_prior


def backward_suffix(state):
    empty_state = jnp.zeros_like(state)
    inner_later = carried_in(state, "inner", add_terms, empty_state, True)
    row_total = lax.psum(state, "inner")
    return carried_in(row_total, "outer", add_terms, empty_state, True) + inner_later


def per_device(query, key, value, grad_out):
    rows_dev = query.shape[0]
    scaling = HEAD ** (-0.5)
    queries = query.reshape(rows_dev, HEADS, HEAD)
    key_rows = key.reshape(rows_dev, HEADS, HEAD)
    value_rows = value.reshape(rows_dev, HEADS, HEAD)
    line = lax.broadcasted_iota(jnp.int32, (rows_dev, rows_dev), 0)
    column = lax.broadcasted_iota(jnp.int32, (rows_dev, rows_dev), 1)
    causal = (line >= column)[None]
    state = jnp.einsum("thi,thj->hij", key_rows, value_rows, preferred_element_type=jnp.float32)
    prior = forward_prefix(state)
    prior_half = prior.astype(jnp.bfloat16)
    scores = (
        jnp.einsum("thi,shi->hts", queries, key_rows, preferred_element_type=jnp.float32) * scaling
    )
    score_half = jnp.where(causal, scores, 0.0).astype(jnp.bfloat16)
    attended = jnp.einsum(
        "hts,shj->thj", score_half, value_rows, preferred_element_type=jnp.float32
    )
    attended = attended + scaling * jnp.einsum(
        "thi,hij->thj", queries, prior_half, preferred_element_type=jnp.float32
    )
    flat = attended.reshape(rows_dev, HEADS * HEAD)
    inverse = lax.rsqrt(jnp.mean(flat * flat, axis=-1, keepdims=True) + 1e-05)
    normed = flat * inverse
    grads_flat = grad_out.astype(jnp.float32)
    grad_pre = inverse * (
        grads_flat - normed * jnp.mean(grads_flat * normed, axis=-1, keepdims=True)
    )
    grad_half = grad_pre.astype(jnp.bfloat16).reshape(rows_dev, HEADS, HEAD)
    dscores = jnp.einsum("thj,shj->hts", grad_half, value_rows, preferred_element_type=jnp.float32)
    dscore_half = jnp.where(causal, dscores, 0.0).astype(jnp.bfloat16)
    grad_q = jnp.einsum("hts,shi->thi", dscore_half, key_rows, preferred_element_type=jnp.float32)
    grad_q = scaling * (
        grad_q
        + jnp.einsum("thj,hij->thi", grad_half, prior_half, preferred_element_type=jnp.float32)
    )
    grad_state = jnp.einsum("thi,thj->hij", queries, grad_half, preferred_element_type=jnp.float32)
    later = backward_suffix(grad_state)
    later_half = later.astype(jnp.bfloat16)
    grad_k = jnp.einsum("hts,thi->shi", dscore_half, queries, preferred_element_type=jnp.float32)
    grad_k = scaling * (
        grad_k
        + jnp.einsum("shj,hij->shi", value_rows, later_half, preferred_element_type=jnp.float32)
    )
    grad_v = jnp.einsum("hts,thj->shj", score_half, grad_half, preferred_element_type=jnp.float32)
    grad_v = grad_v + scaling * jnp.einsum(
        "shi,hij->shj", key_rows, later_half, preferred_element_type=jnp.float32
    )
    width = HEADS * HEAD
    return (
        normed.astype(jnp.bfloat16),
        grad_q.reshape(rows_dev, width).astype(jnp.bfloat16),
        grad_k.reshape(rows_dev, width).astype(jnp.bfloat16),
        grad_v.reshape(rows_dev, width).astype(jnp.bfloat16),
    )


def solution(mesh):
    placed = (
        P(("grp", "outer", "inner"), None),
        P(("grp", "outer", "inner"), None),
        P(("grp", "outer", "inner"), None),
        P(("grp", "outer", "inner"), None),
    )
    return jax.shard_map(
        per_device,
        mesh=mesh,
        in_specs=placed,
        out_specs=(
            P(("grp", "outer", "inner"), None),
            P(("grp", "outer", "inner"), None),
            P(("grp", "outer", "inner"), None),
            P(("grp", "outer", "inner"), None),
        ),
        check_vma=False,
    )
```

profile of v0, /device:TPU:0, one launch (start us, length us, event | category | flops | bytes accessed | tf_op | source)
XLA Modules:
  0.0 253.9 jit_solution(7140993363098596042)
XLA Ops:
  7.2 1.1 copy.62
  8.6 1.0 fusion.19
  9.6 48.5 %all-gather.11.cloned.1.call-done = f32[32,128,128]{2,1,0:T(8,128)} async-done(((f32[8,128,128]{2,1,0:T(8,128)}), f32[32,128,128]{2,1,0:T(8,128)}) %all-gather.11.cloned.1.call-update) | async-done | bytes 2097168 | tf_op jit(solution)/shard_map/all_gather | solution.py:12
  58.1 0.7 all-reduce.3.cloned.1.call-update
  58.9 39.7 %all-reduce.3.cloned.1.call-done = f32[1,8,128,128]{3,2,1,0:T(8,128)} async-done(((f32[1,8,128,128]{3,2,1,0:T(8,128)}), f32[1,8,128,128]{3,2,1,0:T(8,128)}) %all-reduce.3.cloned.1.call-update) | async-done | bytes 524304 | tf_op jit(solution)/shard_map/psum | solution.py:32
  99.0 3.8 %while.57 = (s32[]{:T(128)}, f32[8,128,128]{2,1,0:T(8,128)S(1)}, s32[]{:T(128)}, f32[4,8,128,128]{3,2,1,0:T(8,128)}, s32[]{:T(128)}, /*index=5*/s32[]{:T(128)}) while((s32[]{:T(128)}, f32[8,128,128]{2,1,0:T(8,128)S(1)}, s32[]{:T(128)}, f32[4,8,128,128]{3,2,1,0:T(8,128)}, s32[]{:T(128)}, /*index=5*/s32[]{:T(128)}) %tuple.146), condition=%wide.region_4.5_spmd.clone, body=%wide.region_3.4_spmd.clone.sunk | while | flops 393220 | bytes 1572957 | solution.py:22
  99.1 1.2 add_select_fusion.9
  100.3 1.2 add_select_fusion.9
  101.6 1.2 add_select_fusion.9
  102.8 19.8 %all-gather.7.cloned.1.call-done = f32[4,8,128,128]{3,2,1,0:T(8,128)} async-done(((f32[1,8,128,128]{3,2,1,0:T(8,128)}), f32[4,8,128,128]{3,2,1,0:T(8,128)}) %all-gather.7.cloned.1.call-update) | async-done | bytes 2097168 | tf_op jit(solution)/shard_map/all_gather | solution.py:12
  122.6 3.7 %while.56 = (s32[]{:T(128)}, f32[8,128,128]{2,1,0:T(8,128)S(1)}, s32[]{:T(128)}, f32[4,8,128,128]{3,2,1,0:T(8,128)}, s32[]{:T(128)}, /*index=5*/s32[]{:T(128)}) while((s32[]{:T(128)}, f32[8,128,128]{2,1,0:T(8,128)S(1)}, s32[]{:T(128)}, f32[4,8,128,128]{3,2,1,0:T(8,128)}, s32[]{:T(128)}, /*index=5*/s32[]{:T(128)}) %tuple.122), condition=%wide.region_2.3_spmd.clone, body=%wide.region_1.2_spmd.clone.sunk | while | flops 393220 | bytes 1572957 | solution.py:22
  122.6 1.2 add_select_fusion.8
  123.9 1.2 add_select_fusion.8
  125.1 1.2 add_select_fusion.8
  127.6 0.9 fusion.15
  128.9 1.0 copy.48
  129.9 0.5 all-reduce.5.cloned.1.call-update
  130.5 0.5 all-gather.13.cloned.1.call-update
  131.1 40.3 %all-reduce.5.cloned.1.call-done = f32[1,8,128,128]{2,3,1,0:T(8,128)} async-done(((f32[1,8,128,128]{2,3,1,0:T(8,128)}), f32[1,8,128,128]{2,3,1,0:T(8,128)}) %all-reduce.5.cloned.1.call-update) | async-done | bytes 524304 | tf_op jit(solution)/shard_map/psum | solution.py:39
  171.4 2.0 copy.47
  174.3 0.9 copy.53
  175.2 1.0 fusion.38
  176.2 1.1 convolution_bitcast_fusion
  177.3 41.0 %all-gather.13.cloned.1.call-done = f32[32,128,128]{2,1,0:T(8,128)} async-done(((f32[8,128,128]{2,1,0:T(8,128)}), f32[32,128,128]{2,1,0:T(8,128)}) %all-gather.13.cloned.1.call-update) | async-done | bytes 2097168 | tf_op jit(solution)/shard_map/all_gather | solution.py:12
  218.3 1.7 rev.7
  220.0 0.6 while.59
  220.6 20.5 %all-gather.9.cloned.1.call-done = f32[4,8,128,128]{3,2,1,0:T(8,128)} async-done(((f32[1,8,128,128]{3,2,1,0:T(8,128)}), f32[4,8,128,128]{3,2,1,0:T(8,128)}) %all-gather.9.cloned.1.call-update) | async-done | bytes 2097168 | tf_op jit(solution)/shard_map/all_gather | solution.py:12
  241.1 1.7 rev.6
  242.9 0.6 while.58
  243.5 1.5 fusion.9
  245.0 0.9 copy.55
  246.2 0.9 copy.54
  (48 shorter events, 4.6 us)
Async XLA Ops:
  7.2 1.4 copy-start
  7.2 91.5 %copy-start.4 = (bf16[128,1024]{1,0:T(8,128)(2,1)S(1)}, bf16[128,1024]{1,0:T(8,128)(2,1)}, u32[]{:S(2)}) copy-start(bf16[128,1024]{1,0:T(8,128)(2,1)} %param.13) | copy-start | bytes 786436
  7.2 91.5 %copy-start.2 = (bf16[128,1024]{1,0:T(8,128)(2,1)S(1)}, bf16[128,1024]{1,0:T(8,128)(2,1)}, u32[]{:S(2)}) copy-start(bf16[128,1024]{1,0:T(8,128)(2,1)} %param.12) | copy-start | bytes 786436
  7.2 50.9 %all-gather.11.cloned.1.call-start = ((), (), s32[]{:S(2)}) async-start(), calls=%async_computation.4 | async-start | bytes 2621440 | tf_op jit(solution)/shard_map/all_gather | solution.py:12
  58.1 40.5 %all-reduce.3.cloned.1.call-start = ((), (), s32[]{:S(2)}) async-start(), calls=%async_computation | async-start | bytes 1048576 | tf_op jit(solution)/shard_map/psum | solution.py:32
  58.9 63.7 %all-gather.7.cloned.1.call-start = ((), (), s32[]{:S(2)}) async-start(), calls=%async_computation.1 | async-start | bytes 2621440 | tf_op jit(solution)/shard_map/all_gather | solution.py:12
  126.4 1.0 copy-start.5
  128.9 1.0 copy-start.1
  129.9 41.5 %all-reduce.5.cloned.1.call-start = ((), (), s32[]{:S(2)}) async-start(), calls=%async_computation.2 | async-start | bytes 1048576 | tf_op jit(solution)/shard_map/psum | solution.py:39
  130.5 87.9 %all-gather.13.cloned.1.call-start = ((), (), s32[]{:S(2)}) async-start(), calls=%async_computation.5 | async-start | bytes 2621440 | tf_op jit(solution)/shard_map/all_gather | solution.py:12
  131.0 110.1 %all-gather.9.cloned.1.call-start = ((), (), s32[]{:S(2)}) async-start(), calls=%async_computation.3 | async-start | bytes 2621440 | tf_op jit(solution)/shard_map/all_gather | solution.py:12
  243.5 2.4 copy-start.3
Sparse Core Ops, SparseCore 0:
  9.7 48.3 all-gather.10
  61.3 37.3 all-reduce.2
  100.2 22.3 all-gather.6
  132.7 38.6 all-reduce.4
  172.8 45.4 all-gather.12
  219.7 21.3 all-gather.8
where the time goes:
time: 254 us
  waiting for transfers between devices  212 us (83%)
  between operations  14.4 us (6%)
  local copies, waits for them, and re-layouts  10.8 us (4%)
  other arithmetic  9.62 us (4%)
  matrix products  6.99 us (3%)
    all_gather x4, waiting for transfers between devices, carried_in(): pieces = lax.all_gather(value, axis)  130 us
    psum x1, waiting for transfers between devices, backward_suffix(): row_total = lax.psum(state, 'inner')  40.3 us
    psum x1, waiting for transfers between devices, forward_prefix(): row_total = lax.psum(state, 'inner')  39.7 us
    select_n x12, other arithmetic, lap(): return jnp.where(position < mine, longer, running)  8.37 us
  transfers between devices with their start and end apart: 6, of which 6 were waited for; matrix products, arithmetic and copies ran while one was open for 5% of the time, Pallas kernels for 0%

commit v1 on v0

--- a/solution.py
+++ b/solution.py
@@ -29,7 +29,7 @@
 def forward_prefix(state):
     empty_state = jnp.zeros_like(state)
     inner_prior = carried_in(state, "inner", add_terms, empty_state, False)
-    row_total = lax.psum(state, "inner")
+    row_total = jnp.sum(lax.all_gather(state, "inner"), 0)
     return carried_in(row_total, "outer", add_terms, empty_state, False) + inner_prior
 
 

time: 254 us -> 214 us (0.84)
  waiting for transfers between devices: 212 us -> 169 us
  other arithmetic: 9.62 us -> 12.2 us
    all_gather x4 -> x3, waiting for transfers between devices: 130 us -> 78.9 us  [carried_in(): pieces = lax.all_gather(value, axis)]
    all_gather x0 -> x1, waiting for transfers between devices: none -> 48.5 us  [forward_prefix(): row_total = jnp.sum(lax.all_gather(state, 'inner'), 0)]
    psum x1 -> x0, waiting for transfers between devices: 39.7 us -> none  [forward_prefix(): row_total = lax.psum(state, 'inner')]
    reduce_sum x0 -> x1, other arithmetic: none -> 2.55 us  [forward_prefix(): row_total = jnp.sum(lax.all_gather(state, 'inner'), 0)]
  transfers between devices with their start and end apart: 6 -> 5, of which waited for: 6 -> 5; matrix products, arithmetic and copies ran while one was open for 5% -> 6% of each run, Pallas kernels for 0% -> 0%
where the time goes in v1:
time: 214 us; the launch traced here: 213 us
  waiting for transfers between devices  169 us (79%)
  between operations  14 us (7%)
  other arithmetic  12.2 us (6%)
  local copies, waits for them, and re-layouts  10.7 us (5%)
  matrix products  6.98 us (3%)
    all_gather x3, waiting for transfers between devices, carried_in(): pieces = lax.all_gather(value, axis)  78.9 us
    all_gather x1, waiting for transfers between devices, forward_prefix(): row_total = jnp.sum(lax.all_gather(state, 'inner'), 0)  48.5 us
    psum x1, waiting for transfers between devices, backward_suffix(): row_total = lax.psum(state, 'inner')  40.5 us
    select_n x12, other arithmetic, lap(): return jnp.where(position < mine, longer, running)  8.37 us
  transfers between devices with their start and end apart: 5, of which 5 were waited for; matrix products, arithmetic and copies ran while one was open for 6% of the time, Pallas kernels for 0%

profile of v1, /device:TPU:0, one launch (start us, length us, event | category | flops | bytes accessed | tf_op | source)
XLA Modules:
  0.0 213.4 jit_solution(11320547761382715132)
XLA Ops:
  7.2 1.0 copy.62
  8.5 1.0 fusion.19
  9.6 48.5 %all-gather.10.cloned.1.call-done = f32[32,128,128]{2,1,0:T(8,128)} async-done(((f32[8,128,128]{2,1,0:T(8,128)}), f32[32,128,128]{2,1,0:T(8,128)}) %all-gather.10.cloned.1.call-update) | async-done | bytes 2097168 | tf_op jit(solution)/shard_map/all_gather | solution.py:32
  58.1 2.6 %reduce_sum.27 = f32[8,128,128]{2,1,0:T(8,128)} reduce(f32[4,8,128,128]{3,2,1,0:T(8,128)} %bitcast.129, f32[]{:T(128)} %constant.104.clone.1), dimensions={0}, to_apply=%region_0.1 | reduce | flops 393216 | bytes 2621444 | tf_op jit(solution)/shard_map/reduce_sum | solution.py:32
  61.1 3.8 %while.57 = (s32[]{:T(128)}, f32[8,128,128]{2,1,0:T(8,128)S(1)}, s32[]{:T(128)}, f32[4,8,128,128]{3,2,1,0:T(8,128)}, s32[]{:T(128)}, /*index=5*/s32[]{:T(128)}) while((s32[]{:T(128)}, f32[8,128,128]{2,1,0:T(8,128)S(1)}, s32[]{:T(128)}, f32[4,8,128,128]{3,2,1,0:T(8,128)}, s32[]{:T(128)}, /*index=5*/s32[]{:T(128)}) %tuple.144), condition=%wide.region_4.5_spmd.clone, body=%wide.region_3.4_spmd.clone.sunk | while | flops 393220 | bytes 1572957 | solution.py:22
  61.1 1.2 add_select_fusion.9
  62.3 1.2 add_select_fusion.9
  63.6 1.2 add_select_fusion.9
  64.8 17.4 %all-gather.12.cloned.1.call-done = f32[32,128,128]{2,1,0:T(8,128)} async-done(((f32[8,128,128]{2,1,0:T(8,128)}), f32[32,128,128]{2,1,0:T(8,128)}) %all-gather.12.cloned.1.call-update) | async-done | bytes 2097168 | tf_op jit(solution)/shard_map/all_gather | solution.py:12
  82.2 3.7 %while.56 = (s32[]{:T(128)}, f32[8,128,128]{2,1,0:T(8,128)S(1)}, s32[]{:T(128)}, f32[4,8,128,128]{3,2,1,0:T(8,128)}, s32[]{:T(128)}, /*index=5*/s32[]{:T(128)}) while((s32[]{:T(128)}, f32[8,128,128]{2,1,0:T(8,128)S(1)}, s32[]{:T(128)}, f32[4,8,128,128]{3,2,1,0:T(8,128)}, s32[]{:T(128)}, /*index=5*/s32[]{:T(128)}) %tuple.145), condition=%wide.region_2.3_spmd.clone, body=%wide.region_1.2_spmd.clone.sunk | while | flops 393220 | bytes 1572957 | solution.py:22
  82.2 1.2 add_select_fusion.8
  83.4 1.2 add_select_fusion.8
  84.7 1.2 add_select_fusion.8
  86.3 0.4 multiply_reduce_fusion
  87.2 0.9 fusion.15
  88.5 1.0 copy.48
  89.5 0.7 all-reduce.2.cloned.1.call-update
  90.2 0.5 all-gather.14.cloned.1.call-update
  90.8 40.5 %all-reduce.2.cloned.1.call-done = f32[1,8,128,128]{2,3,1,0:T(8,128)} async-done(((f32[1,8,128,128]{2,3,1,0:T(8,128)}), f32[1,8,128,128]{2,3,1,0:T(8,128)}) %all-reduce.2.cloned.1.call-update) | async-done | bytes 524304 | tf_op jit(solution)/shard_map/psum | solution.py:39
  131.3 2.0 copy.47
  134.2 0.9 copy.53
  135.1 1.0 fusion.38
  136.1 1.1 convolution_bitcast_fusion
  137.2 41.0 %all-gather.14.cloned.1.call-done = f32[32,128,128]{2,1,0:T(8,128)} async-done(((f32[8,128,128]{2,1,0:T(8,128)}), f32[32,128,128]{2,1,0:T(8,128)}) %all-gather.14.cloned.1.call-update) | async-done | bytes 2097168 | tf_op jit(solution)/shard_map/all_gather | solution.py:12
  178.2 1.7 rev.7
  179.9 0.6 while.59
  180.5 20.5 %all-gather.8.cloned.1.call-done = f32[4,8,128,128]{3,2,1,0:T(8,128)} async-done(((f32[1,8,128,128]{3,2,1,0:T(8,128)}), f32[4,8,128,128]{3,2,1,0:T(8,128)}) %all-gather.8.cloned.1.call-update) | async-done | bytes 2097168 | tf_op jit(solution)/shard_map/all_gather | solution.py:12
  201.0 1.7 rev.6
  202.7 0.6 while.58
  203.4 1.5 fusion.9
  204.9 0.9 copy.55
  206.1 0.9 copy.54
  (46 shorter events, 4.2 us)
Async XLA Ops:
  7.2 1.3 copy-start
  7.2 50.9 %all-gather.10.cloned.1.call-start = ((), (), s32[]{:S(2)}) async-start(), calls=%async_computation.2 | async-start | bytes 2621440 | tf_op jit(solution)/shard_map/all_gather | solution.py:32
  9.5 51.2 %copy-start.2 = (bf16[128,1024]{1,0:T(8,128)(2,1)S(1)}, bf16[128,1024]{1,0:T(8,128)(2,1)}, u32[]{:S(2)}) copy-start(bf16[128,1024]{1,0:T(8,128)(2,1)} %param.12) | copy-start | bytes 786436
  9.5 51.2 %copy-start.4 = (bf16[128,1024]{1,0:T(8,128)(2,1)S(1)}, bf16[128,1024]{1,0:T(8,128)(2,1)}, u32[]{:S(2)}) copy-start(bf16[128,1024]{1,0:T(8,128)(2,1)} %param.13) | copy-start | bytes 786436
  9.6 72.6 %all-gather.12.cloned.1.call-start = ((), (), s32[]{:S(2)}) async-start(), calls=%async_computation.3 | async-start | bytes 2621440 | tf_op jit(solution)/shard_map/all_gather | solution.py:12
  86.0 1.0 copy-start.5
  88.5 1.0 copy-start.1
  89.5 41.8 %all-reduce.2.cloned.1.call-start = ((), (), s32[]{:S(2)}) async-start(), calls=%async_computation | async-start | bytes 1048576 | tf_op jit(solution)/shard_map/psum | solution.py:39
  90.2 88.0 %all-gather.14.cloned.1.call-start = ((), (), s32[]{:S(2)}) async-start(), calls=%async_computation.4 | async-start | bytes 2621440 | tf_op jit(solution)/shard_map/all_gather | solution.py:12
  90.8 110.2 %all-gather.8.cloned.1.call-start = ((), (), s32[]{:S(2)}) async-start(), calls=%async_computation.1 | async-start | bytes 2621440 | tf_op jit(solution)/shard_map/all_gather | solution.py:12
  203.3 2.4 %copy-start.3 = (f32[128,8,128]{0,2,1:T(8,128)S(1)}, f32[128,8,128]{0,2,1:T(8,128)}, u32[]{:S(2)}) copy-start(f32[128,8,128]{0,2,1:T(8,128)} %convolution_bitcast_fusion) | copy-start | bytes 1572868
Sparse Core Ops, SparseCore 0:
  9.7 48.3 all-gather.9
  60.8 21.3 all-gather.11
  92.6 38.6 all-reduce.1
  132.7 45.4 all-gather.13
  179.6 21.3 all-gather.7
